TPU v7x, 512 devices: a whole 4x8x8 slice. The times are simulated.
512 devices in a mesh: grp: 16 (over z, core), shard: 32 (over x, y).
Axes of the slice: x: 4, y: 8, z: 8, core: 2. Of those that a mesh axis runs over, the one named last changes fastest.
Arguments:
- src_rows: bfloat16 [128, 128, 5376], P('grp', 'shard'), may hold values from -6 to 6
- src_act: bfloat16 [128, 128], P('grp', 'shard'), may hold values from 0.29882812 to 3
- encoder: bfloat16 [16, 32, 3, 5376, 128], P('grp', 'shard'), may hold values from -0.078125 to 0.078125
- dest_list: int32 [16, 6], replicated, may hold values from -1 to 127, as said below
- pair_list: int32 [16, 32, 18, 2], P('grp', 'shard'), may hold values from 0 to 5, as said below
- pair_count: int32 [16, 32], P('grp', 'shard'), may hold values from 1 to 18, as said below
Outputs:
- edges: bfloat16 [16, 32, 18, 128, 128], P('grp', 'shard')
Inputs may be any that keep to these rules, and one draw needn't show every extreme that they name: `dest_list`: row g holds between 3 and 6 source blocks followed by -1; the blocks of one row come from distinct source groups (block // 8); some row is full. `pair_list`: entries are (slot, encoder block) with slot < 6 and block < 3; the first pair_count entries of a device are distinct pairs whose slot holds a block of its group. `pair_count`: at most 3 times the number of blocks of the device's group; some device has 18.
All inputs are finite; a program needn't handle non-finite values.
Results may differ from a plain program's by a relative error of at most 0.001.
Values may be sent and summed in bfloat16 or wider, within the bound.
No kernel may reach another device: no remote copies, remote signals or barrier semaphores. Data moves between devices by JAX's collectives and lax.ppermute only.
A program may use at most 64 MiB of HBM per device.

v0:
```python
import jax
import jax.numpy as jnp
from jax import lax
from jax.sharding import PartitionSpec as P


def local(src_rows, src_act, encoder, dest_list, pair_list, pair_count):
    my_group = lax.axis_index("grp")
    my_list = lax.dynamic_index_in_dim(dest_list, my_group, 0, keepdims=False)
    is_valid = my_list >= 0
    picked = jnp.maximum(my_list, 0)
    all_rows, all_scale = (
        lax.all_gather(src_rows, "grp", axis=0, tiled=True),
        lax.all_gather(src_act, "grp", axis=0, tiled=True),
    )
    slot_rows = jnp.take(all_rows, picked, axis=0)
    slot_scale = jnp.take(all_scale, picked, axis=0)
    slot_rows = jnp.where(is_valid[:, None, None], slot_rows, jnp.zeros((), slot_rows.dtype))
    slot_scale = jnp.where(is_valid[:, None], slot_scale, jnp.zeros((), slot_scale.dtype))
    full_rows, full_scale = (
        lax.all_gather(slot_rows, "shard", axis=1, tiled=True),
        lax.all_gather(slot_scale, "shard", axis=1, tiled=True),
    )
    weights = encoder[0, 0]
    dev_pairs = pair_list[0, 0]
    slot_ids = dev_pairs[:, 0]
    block_ids = dev_pairs[:, 1]
    amount = pair_count[0, 0]
    slots_total = full_rows.shape[0]
    tile_rows = full_rows.shape[1]
    width = full_rows.shape[2]
    enc_count = weights.shape[0]
    tile_cols = weights.shape[2]
    pair_total = dev_pairs.shape[0]
    stacked = full_rows.reshape(slots_total * tile_rows, width)
    products = jnp.einsum("rd,edc->rec", stacked, weights, preferred_element_type=jnp.float32)
    products = products.reshape(slots_total, tile_rows, enc_count, tile_cols)
    chosen = products[slot_ids, :, block_ids, :]
    scales = jnp.take(full_scale, slot_ids, axis=0).astype(jnp.float32)
    is_live = jnp.arange(pair_total) < amount
    result = jnp.where(
        is_live[:, None, None], scales[:, :, None] * chosen, jnp.zeros((), jnp.float32)
    ).astype(jnp.bfloat16)
    return result[None, None]


def solution(mesh):
    return jax.shard_map(
        local,
        mesh=mesh,
        in_specs=(
            P("grp", "shard", None),
            P("grp", "shard"),
            P("grp", "shard", None, None, None),
            P(),
            P("grp", "shard", None, None),
            P("grp", "shard"),
        ),
        out_specs=P("grp", "shard", None, None, None),
        check_vma=False,
    )
```

profile of v0, /device:TPU:1, one launch (start us, length us, event | category | flops | bytes accessed | tf_op | source)
XLA Modules:
  0.0 197.3 jit_solution(8817233090064426488)
XLA Ops:
  6.5 0.0 copy-start
  6.5 0.0 all-gather.5.cloned.1.call-start
  6.5 0.7 all-gather.5.cloned.1.call-update
  7.3 0.0 copy-start.1
  7.3 0.0 all-gather.7.cloned.1.call-start
  7.3 0.9 maximum_reduce_fusion
  8.2 0.9 compare_reduce_fusion.1
  9.1 53.5 %all-gather.5.cloned.1.call-done = bf16[128,4,5376]{2,1,0:T(4,128)(2,1)} async-done(((bf16[8,4,5376]{2,1,0:T(4,128)(2,1)}), bf16[128,4,5376]{2,1,0:T(4,128)(2,1)}) %all-gather.5.cloned.1.call-update) | async-done | bytes 5505040 | tf_op jit(solution)/shard_map/all_gather | solution.py:13
  62.6 3.3 %gather_fusion.2 = bf16[6,4,5376]{2,1,0:T(4,128)(2,1)S(1)} fusion(bf16[128,4,5376]{2,1,0:T(4,128)(2,1)} %all-gather.5.cloned.1.call-done, s32[1024]{0:T(1024)S(1)} %pad_clamp_fusion.1), kind=kCustom, calls=%fused_computation.2 | custom fusion | bytes 516120 | tf_op jit(solution)/shard_map/jit(_take)/gather | solution.py:16
  65.9 0.2 select_select_fusion
  66.2 0.8 copy.16
  66.9 0.0 all-gather.7.cloned.1.call-update
  67.0 0.0 copy-done
  67.0 16.3 %all-gather = bf16[16,8,4]{1,2,0:T(4,128)(2,1)S(1)} all-gather(bf16[1,8,4]{1,2,0:T(4,128)(2,1)S(1)} %bitcast.32), channel_id=1, replica_groups=mesh['grp'=16,'shard'=32] {'grp'}, dimensions={0}, use_global_device_ids=true | all-gather | bytes 1088 | tf_op jit(solution)/shard_map/all_gather | solution.py:14
  83.3 0.2 copy.13
  83.5 0.6 gather_fusion
  84.0 0.1 select_bitcast_fusion
  84.1 0.1 copy.14
  84.2 33.3 %all-gather.1 = bf16[32,4,6]{2,1,0:T(4,128)(2,1)S(1)} all-gather(bf16[1,4,6]{2,1,0:T(4,128)(2,1)S(1)} %bitcast.31), channel_id=1, replica_groups=mesh['grp'=16,'shard'=32] {'shard'}, dimensions={0}, use_global_device_ids=true | all-gather | bytes 1584 | tf_op jit(solution)/shard_map/all_gather | solution.py:22
  117.5 0.1 copy.19
  118.2 0.0 copy-done.1
  118.3 0.6 gather_fusion.1
  118.9 0.1 select_convert_fusion
  118.9 61.3 %all-gather.7.cloned.1.call-done = bf16[6,128,5376]{2,0,1:T(8,128)(2,1)} async-done(((bf16[6,4,5376]{2,0,1:T(8,128)(2,1)}), bf16[6,128,5376]{2,0,1:T(8,128)(2,1)}) %all-gather.7.cloned.1.call-update) | async-done | bytes 8257552 | tf_op jit(solution)/shard_map/all_gather | solution.py:21
  180.2 8.4 %fusion = f32[6,128,3,128]{3,1,2,0:T(8,128)S(1)} fusion(bf16[6,128,5376,1]{2,0,1,3:T(8,128)(2,1)} %bitcast.35, bf16[1,1,3,5376,128]{4,3,2,1,0:T(8,128)(2,1)} %param.8), kind=kOutput, calls=%fused_computation.4 | convolution fusion | flops 3170893824 | bytes 13565952 | tf_op jit(solution)/shard_map/rd,edc->rec/dot_general | solution.py:36
  188.6 0.7 gather_fusion.3
  189.3 1.2 fusion.4
  (5 shorter events, 0.0 us)
Async XLA Ops:
  6.5 60.4 %copy-start = (bf16[8,4]{0,1:T(4,128)(2,1)S(1)}, bf16[8,4]{0,1:T(4,128)(2,1)}, u32[]{:S(2)}) copy-start(bf16[8,4]{0,1:T(4,128)(2,1)} %param.7) | copy-start | bytes 196
  6.5 56.1 %all-gather.5.cloned.1.call-start = ((), (), s32[]{:S(2)}) async-start(), calls=%async_computation | async-start | bytes 5849088 | tf_op jit(solution)/shard_map/all_gather | solution.py:13
  7.3 111.0 %copy-start.1 = (s32[1,1,18,2]{2,3,1,0:T(2,128)S(1)}, s32[1,1,18,2]{2,3,1,0:T(2,128)}, u32[]{:S(2)}) copy-start(s32[1,1,18,2]{2,3,1,0:T(2,128)} %param.10) | copy-start | bytes 436
  7.3 172.9 %all-gather.7.cloned.1.call-start = ((), (), s32[]{:S(2)}) async-start(), calls=%async_computation.1 | async-start | bytes 11354112 | tf_op jit(solution)/shard_map/all_gather | solution.py:21
Sparse Core Ops, SparseCore 0:
  9.5 53.1 all-gather.4
  67.1 113.0 all-gather.6
where the time goes:
time: 198 us; the launch traced here: 197 us
  waiting for transfers between devices  115 us (58%)
  blocking collectives  49.6 us (25%)
  between operations  14.2 us (7%)
  matrix products  8.42 us (4%)
  local copies, waits for them, and re-layouts  6.26 us (3%)
  other arithmetic  3.4 us (2%)
    all_gather x1, waiting for transfers between devices, local(): lax.all_gather(slot_rows, 'shard', axis=1, tiled=True)  61.3 us
    all_gather x1, waiting for transfers between devices, local(): lax.all_gather(src_rows, 'grp', axis=0, tiled=True)  53.5 us
    all_gather x1, blocking collectives, local(): lax.all_gather(slot_scale, 'shard', axis=1, tiled=True)  33.3 us
    all_gather x1, blocking collectives, local(): lax.all_gather(src_act, 'grp', axis=0, tiled=True)  16.3 us
    dot_general x1, matrix products, local(): jnp.einsum('rd,edc->rec', stacked, weights, preferred_element_type=jnp.fl...  8.42 us
  transfers between devices with their start and end apart: 2, of which 2 were waited for; matrix products, arithmetic and copies ran while one was open for 2% of the time, Pallas kernels for 0%

commit v1 on v0

--- a/solution.py
+++ b/solution.py
@@ -1,7 +1,39 @@
+import functools
 import jax
 import jax.numpy as jnp
 from jax import lax
 from jax.sharding import PartitionSpec as P
+
+
+def pack_the_columns(own_rows, mesh_ax, dim_no):
+    current_value, piece_now, inter = (
+        lax.psum(1, axis_name=mesh_ax),
+        lax.axis_index(mesh_ax),
+        own_rows.shape[dim_no],
+    )
+    series = list(map(lambda h: (h, (h + 1) % current_value), range(current_value)))
+    lanes = list(map(lambda h: (h, (h - 1) % current_value), range(current_value)))
+    later = jnp.zeros(
+        (*own_rows.shape[:dim_no], current_value * inter, *own_rows.shape[dim_no + 1 :]),
+        own_rows.dtype,
+    )
+    later = lax.dynamic_update_slice_in_dim(later, own_rows, piece_now * inter, axis=dim_no)
+    formed = outer = own_rows
+    b_now = current_value // 2
+    for q in tuple(range(1, b_now + 1)):
+        formed = lax.ppermute(formed, axis_name=mesh_ax, perm=series)
+        later = lax.dynamic_update_slice_in_dim(
+            later, formed, (piece_now - q) % current_value * inter, axis=dim_no
+        )
+        if q < current_value - b_now:
+            outer = lax.ppermute(outer, axis_name=mesh_ax, perm=lanes)
+            later = lax.dynamic_update_slice_in_dim(
+                later, outer, (piece_now + q) % current_value * inter, axis=dim_no
+            )
+    return later
+
+
+create_turns = functools.partial(pack_the_columns, mesh_ax="grp", dim_no=0)
 
 
 def local(src_rows, src_act, encoder, dest_list, pair_list, pair_count):
@@ -10,7 +42,7 @@
     is_valid = my_list >= 0
     picked = jnp.maximum(my_list, 0)
     all_rows, all_scale = (
-        lax.all_gather(src_rows, "grp", axis=0, tiled=True),
+        create_turns(src_rows),
         lax.all_gather(src_act, "grp", axis=0, tiled=True),
     )
     slot_rows = jnp.take(all_rows, picked, axis=0)

time: 198 us -> 213 us (1.076)
  waiting for transfers between devices: 115 us -> 69 us
  starting transfers between devices: 0.04 us -> 40.9 us
  local copies, waits for them, and re-layouts: 6.26 us -> 23.8 us
  blocking collectives: 49.6 us -> 55 us
    all_gather x1 -> x0, waiting for transfers between devices: 53.5 us -> none  [local(): lax.all_gather(src_rows, 'grp', axis=0, tiled=True)]
    ppermute x0 -> x15, starting transfers between devices: none -> 40.9 us  [the longest x7 35.2 us: pack_the_columns(): outer = lax.ppermute(outer, axis_name=mesh_ax, perm=lanes)]
    dynamic_update_slice x0 -> x16, local copies, waits for them, and re-layouts: none -> 13.7 us  [the longest x8 6.81 us: pack_the_columns(): lax.dynamic_update_slice_in_dim(later, formed, (piece_now - q) % current_...]
    ppermute x0 -> x15, waiting for transfers between devices: none -> 5.69 us  [the longest x8 5.62 us: pack_the_columns(): formed = lax.ppermute(formed, axis_name=mesh_ax, perm=series)]
    all_gather x1, blocking collectives: 16.3 us -> 20.8 us  [local(): lax.all_gather(src_act, 'grp', axis=0, tiled=True)]
    broadcast_in_dim x0 -> x1, local copies, waits for them, and re-layouts: none -> 3.82 us  [pack_the_columns(): jnp.zeros((*own_rows.shape[:dim_no], current_value * inter, *own_rows.sha...]
  transfers between devices with their start and end apart: 2 -> 16, of which waited for: 2 -> 2; matrix products, arithmetic and copies ran while one was open for 2% -> 9% of each run, Pallas kernels for 0% -> 0%
where the time goes in v1:
time: 213 us
  waiting for transfers between devices  69 us (32%)
  blocking collectives  55 us (26%)
  starting transfers between devices  40.9 us (19%)
  local copies, waits for them, and re-layouts  23.8 us (11%)
  between operations  14.2 us (7%)
  matrix products  8.42 us (4%)
    all_gather x1, waiting for transfers between devices, local(): lax.all_gather(slot_rows, 'shard', axis=1, tiled=True)  63.3 us
    ppermute x7, starting transfers between devices, pack_the_columns(): outer = lax.ppermute(outer, axis_name=mesh_ax, perm=lanes)  35.2 us
    all_gather x1, blocking collectives, local(): lax.all_gather(slot_scale, 'shard', axis=1, tiled=True)  34.2 us
    all_gather x1, blocking collectives, local(): lax.all_gather(src_act, 'grp', axis=0, tiled=True)  20.8 us
    dot_general x1, matrix products, local(): jnp.einsum('rd,edc->rec', stacked, weights, preferred_element_type=jnp.fl...  8.42 us
    dynamic_update_slice x8, local copies, waits for them, and re-layouts, pack_the_columns(): lax.dynamic_update_slice_in_dim(later, formed, (piece_now - q) % current_...  6.81 us
    dynamic_update_slice x7, local copies, waits for them, and re-layouts, pack_the_columns(): lax.dynamic_update_slice_in_dim(later, outer, (piece_now + q) % current_v...  6.02 us
    ppermute x8, starting transfers between devices, pack_the_columns(): formed = lax.ppermute(formed, axis_name=mesh_ax, perm=series)  5.67 us
  transfers between devices with their start and end apart: 16, of which 2 were waited for; matrix products, arithmetic and copies ran while one was open for 9% of the time, Pallas kernels for 0%

profile of v1, /device:TPU:1, one launch (start us, length us, event | category | flops | bytes accessed | tf_op | source)
XLA Modules:
  0.0 213.3 jit_solution(12422634025235737951)
XLA Ops:
  6.5 3.5 %collective-permute-start = (bf16[8,4,5376]{2,1,0:T(4,128)(2,1)}, bf16[8,4,5376]{2,1,0:T(4,128)(2,1)S(1)}, u32[]{:S(2)}, u32[]{:S(2)}) collective-permute-start(bf16[8,4,5376]{2,1,0:T(4,128)(2,1)} %param.6), channel_id=1, source_target_pairs={{0,32},{32,64},{64,96},{96,128},{128,160},{160,192},{192,224},{224... | collective-permute-start | bytes 1032200 | tf_op jit(solution)/shard_map/ppermute | solution.py:24
  10.0 3.4 %collective-permute-start.1 = (bf16[8,4,5376]{2,1,0:T(4,128)(2,1)}, bf16[8,4,5376]{2,1,0:T(4,128)(2,1)S(1)}, u32[]{:S(2)}, u32[]{:S(2)}) collective-permute-start(bf16[8,4,5376]{2,1,0:T(4,128)(2,1)} %param.6), channel_id=1, source_target_pairs={{0,480},{32,0},{64,32},{96,64},{128,96},{160,128},{192,160},{224,1... | collective-permute-start | bytes 1032200 | tf_op jit(solution)/shard_map/ppermute | solution.py:29
  13.4 3.8 %broadcast_in_dim.80 = bf16[128,4,5376]{2,1,0:T(4,128)(2,1)} broadcast(bf16[]{:T(256)} %constant.145.clone.1), dimensions={} | broadcast | bytes 5505026 | tf_op jit(solution)/shard_map/broadcast_in_dim | solution.py:16
  17.2 0.8 constant_dynamic-update-slice_fusion.15
  18.1 0.2 maximum_reduce_fusion
  18.3 0.2 compare_reduce_fusion.1
  18.5 0.0 collective-permute-done
  18.5 0.0 collective-permute-start.2
  18.5 0.0 collective-permute-done.1
  18.5 3.2 %collective-permute-start.3 = (bf16[8,4,5376]{2,1,0:T(4,128)(2,1)S(1)}, bf16[8,4,5376]{2,1,0:T(4,128)(2,1)S(1)}, u32[]{:S(2)}, u32[]{:S(2)}) collective-permute-start(bf16[8,4,5376]{2,1,0:T(4,128)(2,1)S(1)} %collective-permute-done.1), channel_id=1, source_target_pairs={{0,480},{32,0},{64,32},{96,64},{128,96},{160,128},{192,160},{224,1... | collective-permute-start | bytes 1032200 | tf_op jit(solution)/shard_map/ppermute | solution.py:29
  21.7 0.8 constant_dynamic-update-slice_fusion.14
  22.6 0.9 constant_dynamic-update-slice_fusion.13
  23.4 0.0 collective-permute-done.2
  23.4 1.7 collective-permute-start.4
  25.2 0.0 collective-permute-done.3
  25.2 4.4 %collective-permute-start.5 = (bf16[8,4,5376]{2,1,0:T(4,128)(2,1)S(1)}, bf16[8,4,5376]{2,1,0:T(4,128)(2,1)S(1)}, u32[]{:S(2)}, u32[]{:S(2)}) collective-permute-start(bf16[8,4,5376]{2,1,0:T(4,128)(2,1)S(1)} %collective-permute-done.3), channel_id=1, source_target_pairs={{0,480},{32,0},{64,32},{96,64},{128,96},{160,128},{192,160},{224,1... | collective-permute-start | bytes 1032200 | tf_op jit(solution)/shard_map/ppermute | solution.py:29
  29.6 0.9 constant_dynamic-update-slice_fusion.12
  30.5 0.9 constant_dynamic-update-slice_fusion.11
  31.4 0.0 collective-permute-done.4
  31.4 0.5 collective-permute-start.6
  31.8 0.0 collective-permute-done.5
  31.9 5.6 %collective-permute-start.7 = (bf16[8,4,5376]{2,1,0:T(4,128)(2,1)S(1)}, bf16[8,4,5376]{2,1,0:T(4,128)(2,1)S(1)}, u32[]{:S(2)}, u32[]{:S(2)}) collective-permute-start(bf16[8,4,5376]{2,1,0:T(4,128)(2,1)S(1)} %collective-permute-done.5), channel_id=1, source_target_pairs={{0,480},{32,0},{64,32},{96,64},{128,96},{160,128},{192,160},{224,1... | collective-permute-start | bytes 1032200 | tf_op jit(solution)/shard_map/ppermute | solution.py:29
  37.5 0.8 constant_dynamic-update-slice_fusion.10
  38.4 0.8 constant_dynamic-update-slice_fusion.9
  39.2 0.0 collective-permute-done.6
  39.2 0.0 collective-permute-start.8
  39.2 0.0 collective-permute-done.7
  39.2 6.2 %collective-permute-start.9 = (bf16[8,4,5376]{2,1,0:T(4,128)(2,1)S(1)}, bf16[8,4,5376]{2,1,0:T(4,128)(2,1)S(1)}, u32[]{:S(2)}, u32[]{:S(2)}) collective-permute-start(bf16[8,4,5376]{2,1,0:T(4,128)(2,1)S(1)} %collective-permute-done.7), channel_id=1, source_target_pairs={{0,480},{32,0},{64,32},{96,64},{128,96},{160,128},{192,160},{224,1... | collective-permute-start | bytes 1032200 | tf_op jit(solution)/shard_map/ppermute | solution.py:29
  45.4 0.9 constant_dynamic-update-slice_fusion.8
  46.3 0.9 constant_dynamic-update-slice_fusion.7
  47.1 0.0 collective-permute-done.8
  47.1 0.0 collective-permute-start.10
  47.1 0.0 collective-permute-done.9
  47.1 6.1 %collective-permute-start.11 = (bf16[8,4,5376]{2,1,0:T(4,128)(2,1)S(1)}, bf16[8,4,5376]{2,1,0:T(4,128)(2,1)S(1)}, u32[]{:S(2)}, u32[]{:S(2)}) collective-permute-start(bf16[8,4,5376]{2,1,0:T(4,128)(2,1)S(1)} %collective-permute-done.9), channel_id=1, source_target_pairs={{0,480},{32,0},{64,32},{96,64},{128,96},{160,128},{192,160},{224,1... | collective-permute-start | bytes 1032200 | tf_op jit(solution)/shard_map/ppermute | solution.py:29
  53.3 0.8 constant_dynamic-update-slice_fusion.6
  54.1 0.8 constant_dynamic-update-slice_fusion.5
  55.0 0.0 collective-permute-done.10
  55.0 0.0 collective-permute-start.12
  55.0 0.0 collective-permute-done.11
  55.0 6.2 %collective-permute-start.13 = (bf16[8,4,5376]{2,1,0:T(4,128)(2,1)S(1)}, bf16[8,4,5376]{2,1,0:T(4,128)(2,1)S(1)}, u32[]{:S(2)}, u32[]{:S(2)}) collective-permute-start(bf16[8,4,5376]{2,1,0:T(4,128)(2,1)S(1)} %collective-permute-done.11), channel_id=1, source_target_pairs={{0,480},{32,0},{64,32},{96,64},{128,96},{160,128},{192,160},{224,1... | collective-permute-start | bytes 1032200 | tf_op jit(solution)/shard_map/ppermute | solution.py:29
  61.2 0.8 constant_dynamic-update-slice_fusion.4
  62.0 0.8 constant_dynamic-update-slice_fusion.3
  62.9 0.8 constant_dynamic-update-slice_fusion.2
  63.7 0.0 collective-permute-done.13
  63.7 0.9 constant_dynamic-update-slice_fusion.1
  64.6 5.6 %collective-permute-done.14 = bf16[8,4,5376]{2,1,0:T(4,128)(2,1)S(1)} collective-permute-done((bf16[8,4,5376]{2,1,0:T(4,128)(2,1)S(1)}, bf16[8,4,5376]{2,1,0:T(4,128)(2,1)S(1)}, u32[]{:S(2)}, u32[]{:S(2)}) %collective-permute-start.14) | collective-permute-done | bytes 344096 | tf_op jit(solution)/shard_map/ppermute | solution.py:24
  70.2 0.8 constant_dynamic-update-slice_fusion
  71.0 3.3 %gather_fusion.2 = bf16[6,4,5376]{2,1,0:T(4,128)(2,1)S(1)} fusion(bf16[128,4,5376]{2,1,0:T(4,128)(2,1)} %constant_dynamic-update-slice_fusion, s32[1024]{0:T(1024)S(1)} %pad_clamp_fusion.1), kind=kCustom, calls=%fused_computation.2 | custom fusion | bytes 516120 | tf_op jit(solution)/shard_map/jit(_take)/gather | solution.py:48
  74.4 0.2 select_select_fusion
  74.6 0.8 copy.20
  75.4 0.0 all-gather.4.cloned.1.call-update
  75.4 20.8 %all-gather = bf16[16,8,4]{1,2,0:T(4,128)(2,1)S(1)} all-gather(bf16[1,8,4]{1,2,0:T(4,128)(2,1)S(1)} %bitcast.32), channel_id=1, replica_groups=mesh['grp'=16,'shard'=32] {'grp'}, dimensions={0}, use_global_device_ids=true | all-gather | bytes 1088 | tf_op jit(solution)/shard_map/all_gather | solution.py:46
  96.2 0.2 copy.17
  96.4 0.6 gather_fusion
  96.9 0.1 select_bitcast_fusion
  97.0 0.1 copy.18
  97.1 34.2 %all-gather.1 = bf16[32,4,6]{2,1,0:T(4,128)(2,1)S(1)} all-gather(bf16[1,4,6]{2,1,0:T(4,128)(2,1)S(1)} %bitcast.31), channel_id=1, replica_groups=mesh['grp'=16,'shard'=32] {'shard'}, dimensions={0}, use_global_device_ids=true | all-gather | bytes 1584 | tf_op jit(solution)/shard_map/all_gather | solution.py:54
  131.3 0.1 copy.23
  132.1 0.6 gather_fusion.1
  132.7 0.1 select_convert_fusion
  132.8 63.3 %all-gather.4.cloned.1.call-done = bf16[6,128,5376]{2,0,1:T(8,128)(2,1)} async-done(((bf16[6,4,5376]{2,0,1:T(8,128)(2,1)}), bf16[6,128,5376]{2,0,1:T(8,128)(2,1)}) %all-gather.4.cloned.1.call-update) | async-done | bytes 8257552 | tf_op jit(solution)/shard_map/all_gather | solution.py:53
  196.1 8.4 %fusion = f32[6,128,3,128]{3,1,2,0:T(8,128)S(1)} fusion(bf16[6,128,5376,1]{2,0,1,3:T(8,128)(2,1)} %bitcast.35, bf16[1,1,3,5376,128]{4,3,2,1,0:T(8,128)(2,1)} %param.8), kind=kOutput, calls=%fused_computation.4 | convolution fusion | flops 3170893824 | bytes 13565952 | tf_op jit(solution)/shard_map/rd,edc->rec/dot_general | solution.py:68
  204.5 0.7 gather_fusion.3
  205.2 1.2 fusion.4
  (16 shorter events, 0.1 us)
Async XLA Ops:
  6.5 10.7 %copy-start = (bf16[8,4,5376]{2,1,0:T(4,128)(2,1)S(1)}, bf16[8,4,5376]{2,1,0:T(4,128)(2,1)}, u32[]{:S(2)}) copy-start(bf16[8,4,5376]{2,1,0:T(4,128)(2,1)} %param.6) | copy-start | bytes 1032196
  6.5 11.5 %copy-start.1 = (s32[16,6]{0,1:T(8,128)S(1)}, s32[16,6]{0,1:T(8,128)}, u32[]{:S(2)}) copy-start(s32[16,6]{0,1:T(8,128)} %param.9) | copy-start | bytes 1156
  6.5 189.6 %all-gather.4.cloned.1.call-start = ((), (), s32[]{:S(2)}) async-start(), calls=%async_computation | async-start | bytes 11354112 | tf_op jit(solution)/shard_map/all_gather | solution.py:53
  6.5 11.9 %collective-permute-start = (bf16[8,4,5376]{2,1,0:T(4,128)(2,1)}, bf16[8,4,5376]{2,1,0:T(4,128)(2,1)S(1)}, u32[]{:S(2)}, u32[]{:S(2)}) collective-permute-start(bf16[8,4,5376]{2,1,0:T(4,128)(2,1)} %param.6), channel_id=1, source_target_pairs={{0,32},{32,64},{64,96},{96,128},{128,160},{160,192},{192,224},{224... | collective-permute-start | bytes 1032200 | tf_op jit(solution)/shard_map/ppermute | solution.py:24
  10.0 8.5 %collective-permute-start.1 = (bf16[8,4,5376]{2,1,0:T(4,128)(2,1)}, bf16[8,4,5376]{2,1,0:T(4,128)(2,1)S(1)}, u32[]{:S(2)}, u32[]{:S(2)}) collective-permute-start(bf16[8,4,5376]{2,1,0:T(4,128)(2,1)} %param.6), channel_id=1, source_target_pairs={{0,480},{32,0},{64,32},{96,64},{128,96},{160,128},{192,160},{224,1... | collective-permute-start | bytes 1032200 | tf_op jit(solution)/shard_map/ppermute | solution.py:29
  18.5 5.0 %collective-permute-start.2 = (bf16[8,4,5376]{2,1,0:T(4,128)(2,1)S(1)}, bf16[8,4,5376]{2,1,0:T(4,128)(2,1)S(1)}, u32[]{:S(2)}, u32[]{:S(2)}) collective-permute-start(bf16[8,4,5376]{2,1,0:T(4,128)(2,1)S(1)} %collective-permute-done), channel_id=1, source_target_pairs={{0,32},{32,64},{64,96},{96,128},{128,160},{160,192},{192,224},{224... | collective-permute-start | bytes 1032200 | tf_op jit(solution)/shard_map/ppermute | solution.py:24
  18.5 6.7 %collective-permute-start.3 = (bf16[8,4,5376]{2,1,0:T(4,128)(2,1)S(1)}, bf16[8,4,5376]{2,1,0:T(4,128)(2,1)S(1)}, u32[]{:S(2)}, u32[]{:S(2)}) collective-permute-start(bf16[8,4,5376]{2,1,0:T(4,128)(2,1)S(1)} %collective-permute-done.1), channel_id=1, source_target_pairs={{0,480},{32,0},{64,32},{96,64},{128,96},{160,128},{192,160},{224,1... | collective-permute-start | bytes 1032200 | tf_op jit(solution)/shard_map/ppermute | solution.py:29
  23.4 51.9 %copy-start.2 = (bf16[8,4]{0,1:T(4,128)(2,1)S(1)}, bf16[8,4]{0,1:T(4,128)(2,1)}, u32[]{:S(2)}) copy-start(bf16[8,4]{0,1:T(4,128)(2,1)} %param.7) | copy-start | bytes 196
  23.4 108.6 %copy-start.3 = (s32[1,1,18,2]{2,3,1,0:T(2,128)S(1)}, s32[1,1,18,2]{2,3,1,0:T(2,128)}, u32[]{:S(2)}) copy-start(s32[1,1,18,2]{2,3,1,0:T(2,128)} %param.10) | copy-start | bytes 436
  23.4 7.9 %collective-permute-start.4 = (bf16[8,4,5376]{2,1,0:T(4,128)(2,1)S(1)}, bf16[8,4,5376]{2,1,0:T(4,128)(2,1)S(1)}, u32[]{:S(2)}, u32[]{:S(2)}) collective-permute-start(bf16[8,4,5376]{2,1,0:T(4,128)(2,1)S(1)} %collective-permute-done.2), channel_id=1, source_target_pairs={{0,32},{32,64},{64,96},{96,128},{128,160},{160,192},{192,224},{224... | collective-permute-start | bytes 1032200 | tf_op jit(solution)/shard_map/ppermute | solution.py:24
  25.2 6.7 %collective-permute-start.5 = (bf16[8,4,5376]{2,1,0:T(4,128)(2,1)S(1)}, bf16[8,4,5376]{2,1,0:T(4,128)(2,1)S(1)}, u32[]{:S(2)}, u32[]{:S(2)}) collective-permute-start(bf16[8,4,5376]{2,1,0:T(4,128)(2,1)S(1)} %collective-permute-done.3), channel_id=1, source_target_pairs={{0,480},{32,0},{64,32},{96,64},{128,96},{160,128},{192,160},{224,1... | collective-permute-start | bytes 1032200 | tf_op jit(solution)/shard_map/ppermute | solution.py:29
  31.4 7.8 %collective-permute-start.6 = (bf16[8,4,5376]{2,1,0:T(4,128)(2,1)S(1)}, bf16[8,4,5376]{2,1,0:T(4,128)(2,1)S(1)}, u32[]{:S(2)}, u32[]{:S(2)}) collective-permute-start(bf16[8,4,5376]{2,1,0:T(4,128)(2,1)S(1)} %collective-permute-done.4), channel_id=1, source_target_pairs={{0,32},{32,64},{64,96},{96,128},{128,160},{160,192},{192,224},{224... | collective-permute-start | bytes 1032200 | tf_op jit(solution)/shard_map/ppermute | solution.py:24
  31.9 7.3 %collective-permute-start.7 = (bf16[8,4,5376]{2,1,0:T(4,128)(2,1)S(1)}, bf16[8,4,5376]{2,1,0:T(4,128)(2,1)S(1)}, u32[]{:S(2)}, u32[]{:S(2)}) collective-permute-start(bf16[8,4,5376]{2,1,0:T(4,128)(2,1)S(1)} %collective-permute-done.5), channel_id=1, source_target_pairs={{0,480},{32,0},{64,32},{96,64},{128,96},{160,128},{192,160},{224,1... | collective-permute-start | bytes 1032200 | tf_op jit(solution)/shard_map/ppermute | solution.py:29
  39.2 7.9 %collective-permute-start.8 = (bf16[8,4,5376]{2,1,0:T(4,128)(2,1)S(1)}, bf16[8,4,5376]{2,1,0:T(4,128)(2,1)S(1)}, u32[]{:S(2)}, u32[]{:S(2)}) collective-permute-start(bf16[8,4,5376]{2,1,0:T(4,128)(2,1)S(1)} %collective-permute-done.6), channel_id=1, source_target_pairs={{0,32},{32,64},{64,96},{96,128},{128,160},{160,192},{192,224},{224... | collective-permute-start | bytes 1032200 | tf_op jit(solution)/shard_map/ppermute | solution.py:24
  39.2 7.9 %collective-permute-start.9 = (bf16[8,4,5376]{2,1,0:T(4,128)(2,1)S(1)}, bf16[8,4,5376]{2,1,0:T(4,128)(2,1)S(1)}, u32[]{:S(2)}, u32[]{:S(2)}) collective-permute-start(bf16[8,4,5376]{2,1,0:T(4,128)(2,1)S(1)} %collective-permute-done.7), channel_id=1, source_target_pairs={{0,480},{32,0},{64,32},{96,64},{128,96},{160,128},{192,160},{224,1... | collective-permute-start | bytes 1032200 | tf_op jit(solution)/shard_map/ppermute | solution.py:29
  47.1 7.9 %collective-permute-start.10 = (bf16[8,4,5376]{2,1,0:T(4,128)(2,1)S(1)}, bf16[8,4,5376]{2,1,0:T(4,128)(2,1)S(1)}, u32[]{:S(2)}, u32[]{:S(2)}) collective-permute-start(bf16[8,4,5376]{2,1,0:T(4,128)(2,1)S(1)} %collective-permute-done.8), channel_id=1, source_target_pairs={{0,32},{32,64},{64,96},{96,128},{128,160},{160,192},{192,224},{224... | collective-permute-start | bytes 1032200 | tf_op jit(solution)/shard_map/ppermute | solution.py:24
  47.1 7.9 %collective-permute-start.11 = (bf16[8,4,5376]{2,1,0:T(4,128)(2,1)S(1)}, bf16[8,4,5376]{2,1,0:T(4,128)(2,1)S(1)}, u32[]{:S(2)}, u32[]{:S(2)}) collective-permute-start(bf16[8,4,5376]{2,1,0:T(4,128)(2,1)S(1)} %collective-permute-done.9), channel_id=1, source_target_pairs={{0,480},{32,0},{64,32},{96,64},{128,96},{160,128},{192,160},{224,1... | collective-permute-start | bytes 1032200 | tf_op jit(solution)/shard_map/ppermute | solution.py:29
  55.0 7.9 %collective-permute-start.12 = (bf16[8,4,5376]{2,1,0:T(4,128)(2,1)S(1)}, bf16[8,4,5376]{2,1,0:T(4,128)(2,1)S(1)}, u32[]{:S(2)}, u32[]{:S(2)}) collective-permute-start(bf16[8,4,5376]{2,1,0:T(4,128)(2,1)S(1)} %collective-permute-done.10), channel_id=1, source_target_pairs={{0,32},{32,64},{64,96},{96,128},{128,160},{160,192},{192,224},{224... | collective-permute-start | bytes 1032200 | tf_op jit(solution)/shard_map/ppermute | solution.py:24
  55.0 8.7 %collective-permute-start.13 = (bf16[8,4,5376]{2,1,0:T(4,128)(2,1)S(1)}, bf16[8,4,5376]{2,1,0:T(4,128)(2,1)S(1)}, u32[]{:S(2)}, u32[]{:S(2)}) collective-permute-start(bf16[8,4,5376]{2,1,0:T(4,128)(2,1)S(1)} %collective-permute-done.11), channel_id=1, source_target_pairs={{0,480},{32,0},{64,32},{96,64},{128,96},{160,128},{192,160},{224,1... | collective-permute-start | bytes 1032200 | tf_op jit(solution)/shard_map/ppermute | solution.py:29
  62.9 7.3 %collective-permute-start.14 = (bf16[8,4,5376]{2,1,0:T(4,128)(2,1)S(1)}, bf16[8,4,5376]{2,1,0:T(4,128)(2,1)S(1)}, u32[]{:S(2)}, u32[]{:S(2)}) collective-permute-start(bf16[8,4,5376]{2,1,0:T(4,128)(2,1)S(1)} %collective-permute-done.12), channel_id=1, source_target_pairs={{0,32},{32,64},{64,96},{96,128},{128,160},{160,192},{192,224},{224... | collective-permute-start | bytes 1032200 | tf_op jit(solution)/shard_map/ppermute | solution.py:24
Sparse Core Ops, SparseCore 0:
  75.5 120.5 all-gather.3
